TPU v7x, 256 devices: a whole 4x4x8 slice. The times are simulated.
256 devices in a mesh: row: 8 (over y, core), col: 16 (over x_lo, z), req: 2 (over x_hi).
Axes of the slice: x: 4 (x_hi: 2, x_lo: 2; x = x_hi * 2 + x_lo), y: 4, z: 8, core: 2. Of those that a mesh axis runs over, the one named last changes fastest.
Arguments:
- tokens: bfloat16 [3072, 4096], P(('req', 'row'), 'col'), may hold values from -6 to 6
- up_weight: bfloat16 [4096, 21504], P('col', 'row'), may hold values from -0.09375 to 0.09375
- down_weight: bfloat16 [21504, 4096], P('row', 'col'), may hold values from -0.0390625 to 0.0390625
- pool_states: float32 [192, 2, 128, 64, 128], P('row', 'req', 'col'), may hold values from -6 to 6
- pool_edges: float32 [192, 2, 128, 64, 3], P('row', 'req', 'col'), may hold values from -6 to 6
- finish_ids: int32 [32], replicated, may hold values from 0 to 191, as said below
- slot_perm: int32 [32], replicated, may hold values from 0 to 31, each once
Outputs:
- layer_out: bfloat16 [3072, 4096], P(('req', 'row'), 'col')
- decode_states: float32 [32, 2, 128, 64, 128], P('req', None, 'col', 'row')
- decode_edges: float32 [32, 2, 128, 64, 3], P('req', None, 'col', 'row')
Inputs may be any that keep to these rules, and one draw needn't show every extreme that they name: `finish_ids`: entries are distinct; of the 24 slots r * 24 to (r + 1) * 24 - 1 of one index r of row, at most 8 are named, and exactly 8 for some index. `slot_perm`: every decode slot is named once.
All inputs are finite; a program needn't handle non-finite values.
Results may differ from a plain program's by a relative error of at most 0.0044.
Values may be sent and summed in bfloat16 or wider, within the bound.
No kernel may reach another device: no remote copies, remote signals or barrier semaphores. Data moves between devices by JAX's collectives and lax.ppermute only.
A program may use at most 128 MiB of HBM per device.

v0:
```python
import jax
import jax.numpy as jnp
from jax import lax
from jax.sharding import PartitionSpec as P


def handover(pool_states, pool_edges, finish_ids, slot_perm):
    finished = slot_perm.shape[0]
    numbers = jnp.arange(finished, dtype=jnp.int32)
    matches = slot_perm[None, :] == numbers[:, None]
    inverse = jnp.sum(jnp.where(matches, numbers[None, :], 0), axis=1)
    arrived = (
        lax.all_to_all(pool_states, "row", split_axis=3, concat_axis=0, tiled=True),
        lax.all_to_all(pool_edges, "row", split_axis=3, concat_axis=0, tiled=True),
    )
    wanted_rows = finish_ids[inverse]
    states = arrived[0][wanted_rows]
    edge_rows = arrived[1][wanted_rows]
    return (
        lax.all_to_all(states, "req", split_axis=0, concat_axis=1, tiled=True),
        lax.all_to_all(edge_rows, "req", split_axis=0, concat_axis=1, tiled=True),
    )


def on_device(tokens, up_weight, down_weight, pool_states, pool_edges, finish_ids, slot_perm):
    gathered = lax.all_gather(tokens, "row", axis=0, tiled=True)
    preact = lax.psum_scatter(
        jnp.dot(gathered, up_weight, preferred_element_type=jnp.float32),
        "col",
        scatter_dimension=0,
        tiled=True,
    )
    active = jnp.maximum(preact, 0.0)
    hidden = (active * active).astype(jnp.bfloat16)
    products = jnp.dot(
        lax.all_gather(hidden, "col", axis=0, tiled=True),
        down_weight,
        preferred_element_type=jnp.float32,
    )
    summed = lax.psum_scatter(products, "row", scatter_dimension=0, tiled=True)
    layer_out = (tokens.astype(jnp.float32) + summed).astype(jnp.bfloat16)
    decode_states, decode_edges = handover(pool_states, pool_edges, finish_ids, slot_perm)
    return (layer_out, decode_states, decode_edges)


def solution(mesh):
    in_specs = (
        P(("req", "row"), "col"),
        P("col", "row"),
        P("row", "col"),
        P("row", "req", "col", None, None),
        P("row", "req", "col", None, None),
        P(),
        P(),
    )
    out_specs = (
        P(("req", "row"), "col"),
        P("req", None, "col", "row", None),
        P("req", None, "col", "row", None),
    )
    return jax.shard_map(
        on_device, mesh=mesh, in_specs=in_specs, out_specs=out_specs, check_vma=False
    )
```

profile of v0, /device:TPU:8, one launch (start us, length us, event | category | flops | bytes accessed | tf_op | source)
XLA Modules:
  0.0 376.9 jit_solution(2078895432324157047)
XLA Ops:
  7.2 0.0 copy-start
  7.2 0.0 reduce-scatter.3.cloned.1.call-start
  7.2 14.0 %all_gather.6 = bf16[1536,256]{1,0:T(8,128)(2,1)S(1)} all-gather(bf16[192,256]{1,0:T(8,128)(2,1)} %param.7), channel_id=1, replica_groups=mesh['row'=8,'col'=16,'req'=2] {'row'}, dimensions={0}, use_global_device_ids=true | all-gather | bytes 884736 | tf_op jit(solution)/shard_map/all_gather | solution.py:26
  21.2 0.0 copy-done
  21.2 8.1 %fusion.2 = f32[1536,2688]{1,0:T(8,128)} fusion(bf16[1536,256]{1,0:T(8,128)(2,1)S(1)} %all_gather.6, bf16[256,2688]{1,0:T(8,128)(2,1)S(1)} %copy-done), kind=kOutput, calls=%fused_computation.16 | convolution fusion | flops 2113929216 | bytes 18677760 | tf_op jit(solution)/shard_map/dot_general | solution.py:28
  29.3 0.0 copy-start.4
  29.3 0.0 reduce-scatter.3.cloned.1.call-update
  29.3 0.0 all-gather.2.cloned.1.call-start
  29.3 185.7 %reduce-scatter.3.cloned.1.call-done = f32[96,2688]{1,0:T(8,128)} async-done(((f32[1536,2688]{1,0:T(8,128)}), f32[96,2688]{1,0:T(8,128)}) %reduce-scatter.3.cloned.1.call-update) | async-done | bytes 1032208 | tf_op jit(solution)/shard_map/reduce_scatter | solution.py:27
  215.0 2.1 multiply_convert_fusion
  217.1 0.0 all-gather.2.cloned.1.call-update
  217.1 0.0 copy-done.4
  217.1 0.3 copy.50
  217.4 1.2 reshape.63
  218.7 4.8 %all-to-all-start.2 = ((f32[8,1,4608]{2,1,0:T(1,128)}), f32[8,1,4608]{2,1,0:T(1,128)S(1)}, u32[]{:S(2)}, u32[]{:S(2)}) async-start(f32[8,1,4608]{2,1,0:T(1,128)} %reshape.63), calls=%async_computation.4 | async-start | bytes 294912 | tf_op jit(solution)/shard_map/all_to_all | solution.py:14
  223.5 9.0 %copy.46 = f32[24,1,8,64,128]{4,2,0,1,3:T(8,128)} copy(f32[24,1,8,64,128]{4,3,2,1,0:T(8,128)} %param.10) | data formatting | bytes 12582912 | tf_op args[3]
  232.5 0.0 copy-start.5
  232.5 0.0 all-to-all-done.2
  232.5 4.9 %all-to-all-start = ((f32[24,1,8,64,128]{4,2,0,1,3:T(8,128)}), f32[24,1,8,64,128]{4,2,0,1,3:T(8,128)}, u32[]{:S(2)}, u32[]{:S(2)}) async-start(f32[24,1,8,64,128]{4,2,0,1,3:T(8,128)} %copy.46), calls=%async_computation.2 | async-start | bytes 12582912 | tf_op jit(solution)/shard_map/all_to_all | solution.py:13
  237.5 0.0 copy-start.6
  237.5 0.0 copy-start.2
  237.5 0.2 reduce-scatter.5.cloned.1.call-start
  237.7 77.0 %all-gather.2.cloned.1.call-done = bf16[1536,2688]{1,0:T(8,128)(2,1)} async-done(((bf16[96,2688]{1,0:T(8,128)(2,1)}), bf16[1536,2688]{1,0:T(8,128)(2,1)}) %all-gather.2.cloned.1.call-update) | async-done | bytes 8257552 | tf_op jit(solution)/shard_map/all_gather | solution.py:36
  314.7 0.0 copy-done.5
  314.7 6.9 %fusion.3 = f32[1536,256]{1,0:T(8,128)} fusion(bf16[1536,2688]{1,0:T(8,128)(2,1)} %all-gather.2.cloned.1.call-done, bf16[2688,256]{1,0:T(8,128)(2,1)S(1)} %copy-done.5), kind=kOutput, calls=%fused_computation.17 | convolution fusion | flops 2113929216 | bytes 11206656 | tf_op jit(solution)/shard_map/dot_general | solution.py:35
  321.7 0.0 reduce-scatter.5.cloned.1.call-update
  321.7 0.0 copy-done.6
  321.7 0.1 select_reduce_fusion
  321.8 0.0 copy-done.2
  321.9 0.7 gather_fusion
  322.6 0.5 broadcast.50
  323.1 1.0 reduce
  324.1 0.5 reshape.64
  324.6 0.2 copy.64
  324.8 2.1 copy.58
  326.9 2.2 gather_fusion.2
  329.2 0.8 reshape.65
  330.0 0.0 all-to-all-done
  330.0 4.0 %all-to-all-start.3 = ((f32[2,1,3072]{2,1,0:T(1,128)}), f32[2,1,3072]{2,1,0:T(1,128)S(1)}, u32[]{:S(2)}, u32[]{:S(2)}) async-start(f32[2,1,3072]{2,1,0:T(1,128)} %reshape.65), calls=%async_computation.5 | async-start | bytes 49152 | tf_op jit(solution)/shard_map/all_to_all | solution.py:21
  334.0 6.5 %copy.63 = f32[24,1,8,64,128]{4,3,2,0,1:T(8,128)S(1)} copy(f32[24,1,8,64,128]{4,2,0,1,3:T(8,128)} %all-to-all-done) | data formatting | bytes 12582912 | tf_op jit(solution)/shard_map/all_to_all | solution.py:13
  340.4 0.0 copy-start.1
  340.5 3.6 copy.48
  344.0 0.0 copy-start.3
  344.0 4.5 %gather_fusion.1 = f32[32,8,8,128]{3,2,1,0:T(8,128)} fusion(f32[192,8,8,128]{3,2,1,0:T(8,128)} %bitcast.46, s32[1024]{0:T(1024)S(1)} %pad_clamp_fusion), kind=kCustom, calls=%fused_computation.1 | custom fusion | bytes 2097280 | tf_op jit(solution)/shard_map/gather | solution.py:17
  348.5 0.0 all-to-all-done.3
  348.5 4.8 %all-to-all-start.1 = ((f32[32,1,8,8,128]{4,3,2,1,0:T(8,128)}), f32[32,1,8,8,128]{4,3,2,1,0:T(8,128)S(1)}, u32[]{:S(2)}, u32[]{:S(2)}) async-start(f32[32,1,8,8,128]{4,3,2,1,0:T(8,128)} %bitcast.8), calls=%async_computation.3 | async-start | bytes 2097152 | tf_op jit(solution)/shard_map/all_to_all | solution.py:20
  353.3 0.7 reduce.1
  354.0 0.2 reshape.66
  354.3 0.2 copy.59
  354.5 0.7 copy.57
  355.2 12.5 %all-to-all-done.1 = f32[32,1,8,8,128]{4,3,2,1,0:T(8,128)S(1)} async-done(((f32[32,1,8,8,128]{4,3,2,1,0:T(8,128)}), f32[32,1,8,8,128]{4,3,2,1,0:T(8,128)S(1)}, u32[]{:S(2)}, u32[]{:S(2)}) %all-to-all-start.1) | async-done | bytes 1048608 | tf_op jit(solution)/shard_map/all_to_all | solution.py:20
  367.7 1.0 copy.56
  368.8 0.0 reduce-scatter.5.cloned.1.call-done
  368.8 0.0 copy-done.3
  368.8 1.6 add_convert_fusion
  370.3 0.0 copy-done.1
  (5 shorter events, 0.1 us)
Async XLA Ops:
  7.2 14.0 %copy-start = (bf16[256,2688]{1,0:T(8,128)(2,1)S(1)}, bf16[256,2688]{1,0:T(8,128)(2,1)}, u32[]{:S(2)}) copy-start(bf16[256,2688]{1,0:T(8,128)(2,1)} %param.8) | copy-start | bytes 4128772
  7.2 207.8 %reduce-scatter.3.cloned.1.call-start = ((), (), s32[]{:S(2)}) async-start(), calls=%async_computation.6 | async-start | bytes 17547264 | tf_op jit(solution)/shard_map/reduce_scatter | solution.py:27
  29.3 187.8 %copy-start.4 = (f32[24,1,8,64,3]{3,2,4,1,0:T(8,128)S(1)}, f32[24,1,8,64,3]{3,2,4,1,0:T(8,128)}, u32[]{:S(2)}) copy-start(f32[24,1,8,64,3]{3,2,4,1,0:T(8,128)} %param.11) | copy-start | bytes 442372
  29.3 285.4 %all-gather.2.cloned.1.call-start = ((), (), s32[]{:S(2)}) async-start(), calls=%async_computation.7 | async-start | bytes 8773632 | tf_op jit(solution)/shard_map/all_gather | solution.py:36
  218.7 13.8 %all-to-all-start.2 = ((f32[8,1,4608]{2,1,0:T(1,128)}), f32[8,1,4608]{2,1,0:T(1,128)S(1)}, u32[]{:S(2)}, u32[]{:S(2)}) async-start(f32[8,1,4608]{2,1,0:T(1,128)} %reshape.63), calls=%async_computation.4 | async-start | bytes 294912 | tf_op jit(solution)/shard_map/all_to_all | solution.py:14
  232.5 82.2 %copy-start.5 = (bf16[2688,256]{1,0:T(8,128)(2,1)S(1)}, bf16[2688,256]{1,0:T(8,128)(2,1)}, u32[]{:S(2)}) copy-start(bf16[2688,256]{1,0:T(8,128)(2,1)} %param.9) | copy-start | bytes 4128772
  232.5 97.5 %all-to-all-start = ((f32[24,1,8,64,128]{4,2,0,1,3:T(8,128)}), f32[24,1,8,64,128]{4,2,0,1,3:T(8,128)}, u32[]{:S(2)}, u32[]{:S(2)}) async-start(f32[24,1,8,64,128]{4,2,0,1,3:T(8,128)} %copy.46), calls=%async_computation.2 | async-start | bytes 12582912 | tf_op jit(solution)/shard_map/all_to_all | solution.py:13
  237.5 84.2 %copy-start.6 = (s32[32]{0:T(128)S(1)}, s32[32]{0:T(128)}, u32[]{:S(2)}) copy-start(s32[32]{0:T(128)} %param.13) | copy-start | bytes 388
  237.5 84.4 %copy-start.2 = (s32[32]{0:T(128)S(1)}, s32[32]{0:T(128)}, u32[]{:S(2)}) copy-start(s32[32]{0:T(128)} %param.12) | copy-start | bytes 388
  237.5 131.3 %reduce-scatter.5.cloned.1.call-start = ((), (), s32[]{:S(2)}) async-start(), calls=%async_computation.8 | async-start | bytes 1769472 | tf_op jit(solution)/shard_map/reduce_scatter | solution.py:40
  330.0 18.5 %all-to-all-start.3 = ((f32[2,1,3072]{2,1,0:T(1,128)}), f32[2,1,3072]{2,1,0:T(1,128)S(1)}, u32[]{:S(2)}, u32[]{:S(2)}) async-start(f32[2,1,3072]{2,1,0:T(1,128)} %reshape.65), calls=%async_computation.5 | async-start | bytes 49152 | tf_op jit(solution)/shard_map/all_to_all | solution.py:21
  340.4 29.9 %copy-start.1 = (bf16[256,2688]{1,0:T(8,128)(2,1)S(1)}, bf16[256,2688]{1,0:T(8,128)(2,1)}, u32[]{:S(2)}) copy-start(bf16[256,2688]{1,0:T(8,128)(2,1)} %param.8) | copy-start | bytes 4128772
  344.0 24.7 %copy-start.3 = (bf16[192,256]{1,0:T(8,128)(2,1)S(1)}, bf16[192,256]{1,0:T(8,128)(2,1)}, u32[]{:S(2)}) copy-start(bf16[192,256]{1,0:T(8,128)(2,1)} %param.7) | copy-start | bytes 294916
  348.5 19.2 %all-to-all-start.1 = ((f32[32,1,8,8,128]{4,3,2,1,0:T(8,128)}), f32[32,1,8,8,128]{4,3,2,1,0:T(8,128)S(1)}, u32[]{:S(2)}, u32[]{:S(2)}) async-start(f32[32,1,8,8,128]{4,3,2,1,0:T(8,128)} %bitcast.8), calls=%async_computation.3 | async-start | bytes 2097152 | tf_op jit(solution)/shard_map/all_to_all | solution.py:20
Sparse Core Ops, SparseCore 0:
  29.4 185.5 reduce-scatter.2
  217.4 97.3 all-gather.1
  321.8 30.1 reduce-scatter.4
where the time goes:
time: 378 us; the launch traced here: 377 us
  waiting for transfers between devices  275 us (73%)
  local copies, waits for them, and re-layouts  34.4 us (9%)
  starting transfers between devices  18.8 us (5%)
  matrix products  15 us (4%)
  blocking collectives  14 us (4%)
  between operations  13.9 us (4%)
  other arithmetic  5.52 us (1%)
    reduce_scatter x1, waiting for transfers between devices, on_device(): lax.psum_scatter(jnp.dot(gathered, up_weight, preferred_element_type=jnp....  186 us
    all_gather x1, waiting for transfers between devices, on_device(): lax.all_gather(hidden, 'col', axis=0, tiled=True)  77 us
    unnamed x23, local copies, waits for them, and re-layouts  14 us
    all_gather x1, blocking collectives, on_device(): gathered = lax.all_gather(tokens, 'row', axis=0, tiled=True)  14 us
    all_to_all x1, waiting for transfers between devices, handover(): lax.all_to_all(states, 'req', split_axis=0, concat_axis=1, tiled=True)  12.5 us
    all_to_all x2, local copies, waits for them, and re-layouts, handover(): lax.all_to_all(pool_states, 'row', split_axis=3, concat_axis=0, tiled=True)  10 us
    dot_general x1, matrix products, on_device(): jnp.dot(gathered, up_weight, preferred_element_type=jnp.float32)  8.06 us
  transfers between devices with their start and end apart: 7, of which 3 were waited for; matrix products, arithmetic and copies ran while one was open for 11% of the time, Pallas kernels for 0%

commit v1 on v0

--- a/solution.py
+++ b/solution.py
@@ -1,7 +1,38 @@
+import functools
 import jax
 import jax.numpy as jnp
 from jax import lax
 from jax.sharding import PartitionSpec as P
+
+
+def arrange_view_over_axis(own_rows, k_dim, local_values):
+    val = own_rows.shape
+    odd = own_rows.reshape(
+        *val[:k_dim], local_values, val[k_dim] // local_values, *val[k_dim + 1 :]
+    )
+    return jnp.moveaxis(odd, k_dim, 0)
+
+
+def task_recover(panel, in_dim):
+    panel = jnp.moveaxis(panel, 0, in_dim)
+    p_next = panel.shape
+    return panel.reshape(
+        *p_next[:in_dim], p_next[in_dim] * p_next[in_dim + 1], *p_next[in_dim + 2 :]
+    )
+
+
+def column_supply(local, named_axis, block_here, frame_in):
+    outer, plain = (lax.axis_size(named_axis), lax.axis_index(named_axis))
+    next_value = arrange_view_over_axis(local, block_here, outer)
+    rows = [next_value[plain]]
+    for ix in range(1, outer):
+        part_now = next_value[plain ^ ix]
+        rows.append(lax.ppermute(part_now, named_axis, [(idx, idx ^ ix) for idx in range(outer)]))
+    next_value = jnp.stack(rows)[plain ^ jnp.arange(outer)]
+    return task_recover(next_value, frame_in)
+
+
+group_the_axis_part = functools.partial(column_supply, named_axis="row", block_here=3, frame_in=0)
 
 
 def handover(pool_states, pool_edges, finish_ids, slot_perm):
@@ -11,7 +42,7 @@
     inverse = jnp.sum(jnp.where(matches, numbers[None, :], 0), axis=1)
     arrived = (
         lax.all_to_all(pool_states, "row", split_axis=3, concat_axis=0, tiled=True),
-        lax.all_to_all(pool_edges, "row", split_axis=3, concat_axis=0, tiled=True),
+        group_the_axis_part(pool_edges),
     )
     wanted_rows = finish_ids[inverse]
     states = arrived[0][wanted_rows]

time: 378 us -> 384 us (1.016)
  waiting for transfers between devices: 275 us -> 281 us
    ppermute x0 -> x7, starting transfers between devices: none -> 6.87 us  [column_supply(): lax.ppermute(part_now, named_axis, [(idx, idx ^ ix) for idx in range(oute...]
    ppermute x0 -> x7, waiting for transfers between devices: none -> 4.98 us  [column_supply(): lax.ppermute(part_now, named_axis, [(idx, idx ^ ix) for idx in range(oute...]
    all_to_all x1 -> x0, starting transfers between devices: 4.83 us -> none  [handover(): lax.all_to_all(pool_edges, 'row', split_axis=3, concat_axis=0, tiled=True)]
    unnamed x23 -> x26, local copies, waits for them, and re-layouts: 14 us -> 12.2 us
  transfers between devices with their start and end apart: 7 -> 13, of which waited for: 3 -> 5; matrix products, arithmetic and copies ran while one was open for 11% -> 11% of each run, Pallas kernels for 0% -> 0%
where the time goes in v1:
time: 384 us; the launch traced here: 383 us
  waiting for transfers between devices  281 us (73%)
  local copies, waits for them, and re-layouts  33.3 us (9%)
  starting transfers between devices  21.1 us (5%)
  matrix products  15.3 us (4%)
  blocking collectives  14 us (4%)
  between operations  14 us (4%)
  other arithmetic  4.53 us (1%)
    reduce_scatter x1, waiting for transfers between devices, on_device(): lax.psum_scatter(jnp.dot(gathered, up_weight, preferred_element_type=jnp....  186 us
    all_gather x1, waiting for transfers between devices, on_device(): lax.all_gather(hidden, 'col', axis=0, tiled=True)  77.5 us
    all_gather x1, blocking collectives, on_device(): gathered = lax.all_gather(tokens, 'row', axis=0, tiled=True)  14 us
    all_to_all x1, waiting for transfers between devices, handover(): lax.all_to_all(states, 'req', split_axis=0, concat_axis=1, tiled=True)  12.4 us
    unnamed x26, local copies, waits for them, and re-layouts  12.2 us
    all_to_all x2, local copies, waits for them, and re-layouts, handover(): lax.all_to_all(pool_states, 'row', split_axis=3, concat_axis=0, tiled=True)  10 us
    dot_general x1, matrix products, on_device(): jnp.dot(gathered, up_weight, preferred_element_type=jnp.float32)  8.06 us
  transfers between devices with their start and end apart: 13, of which 5 were waited for; matrix products, arithmetic and copies ran while one was open for 11% of the time, Pallas kernels for 0%

profile of v1, /device:TPU:8, one launch (start us, length us, event | category | flops | bytes accessed | tf_op | source)
XLA Modules:
  0.0 382.8 jit_solution(3809981221154289801)
XLA Ops:
  7.2 0.0 copy-start
  7.2 0.0 reduce-scatter.3.cloned.1.call-start
  7.2 14.0 %all_gather.6 = bf16[1536,256]{1,0:T(8,128)(2,1)S(1)} all-gather(bf16[192,256]{1,0:T(8,128)(2,1)} %param.7), channel_id=1, replica_groups=mesh['row'=8,'col'=16,'req'=2] {'row'}, dimensions={0}, use_global_device_ids=true | all-gather | bytes 884736 | tf_op jit(solution)/shard_map/all_gather | solution.py:57
  21.2 0.0 copy-done
  21.2 8.1 %fusion.3 = f32[1536,2688]{1,0:T(8,128)} fusion(bf16[1536,256]{1,0:T(8,128)(2,1)S(1)} %all_gather.6, bf16[256,2688]{1,0:T(8,128)(2,1)S(1)} %copy-done), kind=kOutput, calls=%fused_computation.34 | convolution fusion | flops 2113929216 | bytes 18677760 | tf_op jit(solution)/shard_map/dot_general | solution.py:59
  29.3 0.0 reduce-scatter.3.cloned.1.call-update
  29.3 0.0 all-gather.2.cloned.1.call-start
  29.3 185.7 %reduce-scatter.3.cloned.1.call-done = f32[96,2688]{1,0:T(8,128)} async-done(((f32[1536,2688]{1,0:T(8,128)}), f32[96,2688]{1,0:T(8,128)}) %reduce-scatter.3.cloned.1.call-update) | async-done | bytes 1032208 | tf_op jit(solution)/shard_map/reduce_scatter | solution.py:58
  215.0 2.1 multiply_convert_fusion
  217.1 0.0 all-gather.2.cloned.1.call-update
  217.1 9.0 %copy.39 = f32[24,1,8,64,128]{4,2,0,1,3:T(8,128)} copy(f32[24,1,8,64,128]{4,3,2,1,0:T(8,128)} %param.10) | data formatting | bytes 12582912 | tf_op args[3]
  226.1 0.0 copy-start.4
  226.1 0.0 copy-start.5
  226.1 5.4 %all-to-all-start = ((f32[24,1,8,64,128]{4,2,0,1,3:T(8,128)}), f32[24,1,8,64,128]{4,2,0,1,3:T(8,128)}, u32[]{:S(2)}, u32[]{:S(2)}) async-start(f32[24,1,8,64,128]{4,2,0,1,3:T(8,128)} %copy.39), calls=%async_computation.2 | async-start | bytes 12582912 | tf_op jit(solution)/shard_map/all_to_all | solution.py:44
  231.5 0.0 reduce-scatter.5.cloned.1.call-start
  231.5 0.0 copy-done.4
  231.5 0.3 copy.43
  231.8 0.1 dynamic-slice_bitcast_fusion
  231.9 0.2 collective-permute-start
  232.1 0.4 collective-permute-start.1
  232.5 1.4 collective-permute-start.2
  233.9 2.1 collective-permute-start.3
  236.0 1.2 collective-permute-start.4
  237.1 0.0 copy-done.5
  237.1 0.1 select_reduce_fusion
  237.2 0.0 copy-start.2
  237.3 77.5 %all-gather.2.cloned.1.call-done = bf16[1536,2688]{1,0:T(8,128)(2,1)} async-done(((bf16[96,2688]{1,0:T(8,128)(2,1)}), bf16[1536,2688]{1,0:T(8,128)(2,1)}) %all-gather.2.cloned.1.call-update) | async-done | bytes 8257552 | tf_op jit(solution)/shard_map/all_gather | solution.py:67
  314.7 7.3 %fusion.4 = f32[1536,256]{1,0:T(8,128)} fusion(bf16[1536,2688]{1,0:T(8,128)(2,1)} %all-gather.2.cloned.1.call-done, bf16[2688,256]{1,0:T(8,128)(2,1)} %param.9), kind=kOutput, calls=%fused_computation.35 | convolution fusion | flops 2113929216 | bytes 11206656 | tf_op jit(solution)/shard_map/dot_general | solution.py:66
  322.0 0.0 reduce-scatter.5.cloned.1.call-update
  322.1 0.0 copy-done.2
  322.1 0.7 gather_fusion
  322.8 0.0 collective-permute-done
  322.8 1.6 collective-permute-start.5
  324.4 0.0 collective-permute-done.1
  324.4 0.1 collective-permute-start.6
  324.6 0.0 collective-permute-done.2
  324.6 0.0 collective-permute-done.3
  324.6 0.0 collective-permute-done.4
  324.6 2.9 collective-permute-done.5
  327.6 2.0 collective-permute-done.6
  329.6 0.6 gather_fusion.2
  330.2 2.1 copy.50
  332.4 2.3 gather_fusion.3
  334.7 0.8 reshape.113
  335.5 0.0 all-to-all-done
  335.5 3.9 %all-to-all-start.2 = ((f32[2,1,3072]{2,1,0:T(1,128)}), f32[2,1,3072]{2,1,0:T(1,128)S(1)}, u32[]{:S(2)}, u32[]{:S(2)}) async-start(f32[2,1,3072]{2,1,0:T(1,128)} %reshape.113), calls=%async_computation.4 | async-start | bytes 49152 | tf_op jit(solution)/shard_map/all_to_all | solution.py:52
  339.5 6.5 %copy.54 = f32[24,1,8,64,128]{4,3,2,0,1:T(8,128)S(1)} copy(f32[24,1,8,64,128]{4,2,0,1,3:T(8,128)} %all-to-all-done) | data formatting | bytes 12582912 | tf_op jit(solution)/shard_map/all_to_all | solution.py:44
  345.9 0.0 copy-start.1
  345.9 3.6 copy.41
  349.5 0.0 copy-start.3
  349.5 4.4 %gather_fusion.1 = f32[32,8,8,128]{3,2,1,0:T(8,128)} fusion(f32[192,8,8,128]{3,2,1,0:T(8,128)} %bitcast.74, s32[1024]{0:T(1024)S(1)} %pad_clamp_fusion.1), kind=kCustom, calls=%fused_computation.1 | custom fusion | bytes 2097280 | tf_op jit(solution)/shard_map/gather | solution.py:48
  353.9 0.0 all-to-all-done.2
  353.9 4.8 %all-to-all-start.1 = ((f32[32,1,8,8,128]{4,3,2,1,0:T(8,128)}), f32[32,1,8,8,128]{4,3,2,1,0:T(8,128)S(1)}, u32[]{:S(2)}, u32[]{:S(2)}) async-start(f32[32,1,8,8,128]{4,3,2,1,0:T(8,128)} %bitcast.8), calls=%async_computation.3 | async-start | bytes 2097152 | tf_op jit(solution)/shard_map/all_to_all | solution.py:51
  358.8 0.5 broadcast.85
  359.3 0.7 reduce
  360.0 0.2 reshape.114
  360.2 0.2 copy.51
  360.5 0.7 copy.49
  361.2 12.4 %all-to-all-done.1 = f32[32,1,8,8,128]{4,3,2,1,0:T(8,128)S(1)} async-done(((f32[32,1,8,8,128]{4,3,2,1,0:T(8,128)}), f32[32,1,8,8,128]{4,3,2,1,0:T(8,128)S(1)}, u32[]{:S(2)}, u32[]{:S(2)}) %all-to-all-start.1) | async-done | bytes 1048608 | tf_op jit(solution)/shard_map/all_to_all | solution.py:51
  373.6 1.0 copy.48
  374.6 0.0 reduce-scatter.5.cloned.1.call-done
  374.6 0.0 copy-done.3
  374.6 1.6 add_convert_fusion
  376.2 0.0 copy-done.1
  (15 shorter events, 0.1 us)
Async XLA Ops:
  7.2 14.0 %copy-start = (bf16[256,2688]{1,0:T(8,128)(2,1)S(1)}, bf16[256,2688]{1,0:T(8,128)(2,1)}, u32[]{:S(2)}) copy-start(bf16[256,2688]{1,0:T(8,128)(2,1)} %param.8) | copy-start | bytes 4128772
  7.2 207.8 %reduce-scatter.3.cloned.1.call-start = ((), (), s32[]{:S(2)}) async-start(), calls=%async_computation.5 | async-start | bytes 17547264 | tf_op jit(solution)/shard_map/reduce_scatter | solution.py:58
  29.3 285.4 %all-gather.2.cloned.1.call-start = ((), (), s32[]{:S(2)}) async-start(), calls=%async_computation.6 | async-start | bytes 8773632 | tf_op jit(solution)/shard_map/all_gather | solution.py:67
  226.1 5.4 %copy-start.4 = (f32[24,1,8,64,3]{3,2,4,1,0:T(8,128)S(1)}, f32[24,1,8,64,3]{3,2,4,1,0:T(8,128)}, u32[]{:S(2)}) copy-start(f32[24,1,8,64,3]{3,2,4,1,0:T(8,128)} %param.11) | copy-start | bytes 442372
  226.1 11.0 %copy-start.5 = (s32[32]{0:T(128)S(1)}, s32[32]{0:T(128)}, u32[]{:S(2)}) copy-start(s32[32]{0:T(128)} %param.13) | copy-start | bytes 388
  226.1 109.4 %all-to-all-start = ((f32[24,1,8,64,128]{4,2,0,1,3:T(8,128)}), f32[24,1,8,64,128]{4,2,0,1,3:T(8,128)}, u32[]{:S(2)}, u32[]{:S(2)}) async-start(f32[24,1,8,64,128]{4,2,0,1,3:T(8,128)} %copy.39), calls=%async_computation.2 | async-start | bytes 12582912 | tf_op jit(solution)/shard_map/all_to_all | solution.py:44
  231.5 143.2 %reduce-scatter.5.cloned.1.call-start = ((), (), s32[]{:S(2)}) async-start(), calls=%async_computation.7 | async-start | bytes 1769472 | tf_op jit(solution)/shard_map/reduce_scatter | solution.py:71
  231.9 90.9 %collective-permute-start = (f32[24,1,8,8,3]{0,3,4,2,1:T(8,128)S(1)}, f32[24,1,8,8,3]{0,3,4,2,1:T(8,128)S(1)}, u32[]{:S(2)}, u32[]{:S(2)}) collective-permute-start(f32[24,1,8,8,3]{0,3,4,2,1:T(8,128)S(1)} %get-tuple-element.24), channel_id=1, source_target_pairs={{0,32},{32,0},{64,96},{96,64},{128,160},{160,128},{192,224},{224,1... | collective-permute-start | bytes 55304 | tf_op jit(solution)/shard_map/ppermute | solution.py:30
  232.1 92.3 %collective-permute-start.1 = (f32[24,1,8,8,3]{0,3,4,2,1:T(8,128)S(1)}, f32[24,1,8,8,3]{0,3,4,2,1:T(8,128)S(1)}, u32[]{:S(2)}, u32[]{:S(2)}) collective-permute-start(f32[24,1,8,8,3]{0,3,4,2,1:T(8,128)S(1)} %get-tuple-element.23), channel_id=1, source_target_pairs={{0,64},{32,96},{64,0},{96,32},{128,192},{160,224},{192,128},{224,1... | collective-permute-start | bytes 55304 | tf_op jit(solution)/shard_map/ppermute | solution.py:30
  232.5 92.0 %collective-permute-start.2 = (f32[24,1,8,8,3]{0,3,4,2,1:T(8,128)S(1)}, f32[24,1,8,8,3]{0,3,4,2,1:T(8,128)S(1)}, u32[]{:S(2)}, u32[]{:S(2)}) collective-permute-start(f32[24,1,8,8,3]{0,3,4,2,1:T(8,128)S(1)} %get-tuple-element.22), channel_id=1, source_target_pairs={{0,96},{32,64},{64,32},{96,0},{128,224},{160,192},{192,160},{224,1... | collective-permute-start | bytes 55304 | tf_op jit(solution)/shard_map/ppermute | solution.py:30
  233.9 90.7 %collective-permute-start.3 = (f32[24,1,8,8,3]{0,3,4,2,1:T(8,128)S(1)}, f32[24,1,8,8,3]{0,3,4,2,1:T(8,128)S(1)}, u32[]{:S(2)}, u32[]{:S(2)}) collective-permute-start(f32[24,1,8,8,3]{0,3,4,2,1:T(8,128)S(1)} %get-tuple-element.21), channel_id=1, source_target_pairs={{0,128},{32,160},{64,192},{96,224},{128,0},{160,32},{192,64},{224,... | collective-permute-start | bytes 55304 | tf_op jit(solution)/shard_map/ppermute | solution.py:30
  236.0 88.7 %collective-permute-start.4 = (f32[24,1,8,8,3]{0,3,4,2,1:T(8,128)S(1)}, f32[24,1,8,8,3]{0,3,4,2,1:T(8,128)S(1)}, u32[]{:S(2)}, u32[]{:S(2)}) collective-permute-start(f32[24,1,8,8,3]{0,3,4,2,1:T(8,128)S(1)} %get-tuple-element.20), channel_id=1, source_target_pairs={{0,160},{32,128},{64,224},{96,192},{128,32},{160,0},{192,96},{224,... | collective-permute-start | bytes 55304 | tf_op jit(solution)/shard_map/ppermute | solution.py:30
  237.2 84.8 %copy-start.2 = (s32[32]{0:T(128)S(1)}, s32[32]{0:T(128)}, u32[]{:S(2)}) copy-start(s32[32]{0:T(128)} %param.12) | copy-start | bytes 388
  322.8 4.7 %collective-permute-start.5 = (f32[24,1,8,8,3]{0,3,4,2,1:T(8,128)S(1)}, f32[24,1,8,8,3]{0,3,4,2,1:T(8,128)S(1)}, u32[]{:S(2)}, u32[]{:S(2)}) collective-permute-start(f32[24,1,8,8,3]{0,3,4,2,1:T(8,128)S(1)} %get-tuple-element.19), channel_id=1, source_target_pairs={{0,192},{32,224},{64,128},{96,160},{128,64},{160,96},{192,0},{224,... | collective-permute-start | bytes 55304 | tf_op jit(solution)/shard_map/ppermute | solution.py:30
  324.4 5.2 %collective-permute-start.6 = (f32[24,1,8,8,3]{0,3,4,2,1:T(8,128)S(1)}, f32[24,1,8,8,3]{0,3,4,2,1:T(8,128)S(1)}, u32[]{:S(2)}, u32[]{:S(2)}) collective-permute-start(f32[24,1,8,8,3]{0,3,4,2,1:T(8,128)S(1)} %get-tuple-element.18), channel_id=1, source_target_pairs={{0,224},{32,192},{64,160},{96,128},{128,96},{160,64},{192,32},{224... | collective-permute-start | bytes 55304 | tf_op jit(solution)/shard_map/ppermute | solution.py:30
  335.5 18.4 %all-to-all-start.2 = ((f32[2,1,3072]{2,1,0:T(1,128)}), f32[2,1,3072]{2,1,0:T(1,128)S(1)}, u32[]{:S(2)}, u32[]{:S(2)}) async-start(f32[2,1,3072]{2,1,0:T(1,128)} %reshape.113), calls=%async_computation.4 | async-start | bytes 49152 | tf_op jit(solution)/shard_map/all_to_all | solution.py:52
  345.9 30.3 %copy-start.1 = (bf16[256,2688]{1,0:T(8,128)(2,1)S(1)}, bf16[256,2688]{1,0:T(8,128)(2,1)}, u32[]{:S(2)}) copy-start(bf16[256,2688]{1,0:T(8,128)(2,1)} %param.8) | copy-start | bytes 4128772
  349.5 25.2 %copy-start.3 = (bf16[192,256]{1,0:T(8,128)(2,1)S(1)}, bf16[192,256]{1,0:T(8,128)(2,1)}, u32[]{:S(2)}) copy-start(bf16[192,256]{1,0:T(8,128)(2,1)} %param.7) | copy-start | bytes 294916
  353.9 19.7 %all-to-all-start.1 = ((f32[32,1,8,8,128]{4,3,2,1,0:T(8,128)}), f32[32,1,8,8,128]{4,3,2,1,0:T(8,128)S(1)}, u32[]{:S(2)}, u32[]{:S(2)}) async-start(f32[32,1,8,8,128]{4,3,2,1,0:T(8,128)} %bitcast.8), calls=%async_computation.3 | async-start | bytes 2097152 | tf_op jit(solution)/shard_map/all_to_all | solution.py:51
Sparse Core Ops, SparseCore 0:
  29.4 185.5 reduce-scatter.2
  217.3 97.3 all-gather.1
  322.2 30.1 reduce-scatter.4
